TPU v7x, 32 devices: a whole 2x2x4 slice. The times are simulated.
32 devices in a mesh: dp: 8 (over z, x), own: 4 (over y, core).
Axes of the slice: x: 2, y: 2, z: 4, core: 2. Of those that a mesh axis runs over, the one named last changes fastest.
Arguments:
- grads_fc: bfloat16 [8, 4, 8, 200, 1600], P('dp', 'own'), may hold values from -180 to 180
- grads_ln: bfloat16 [8, 4, 1600], P('dp'), may hold values from -48 to 48
- grads_emb: bfloat16 [8, 4, 8, 4, 1600], P('dp', 'own'), may hold values from -48 to 48
- weights_fc: bfloat16 [4, 8, 200, 1600], P('own'), may hold values from -0.15625 to 0.15625
- basis: float32 [1600, 256], replicated, may hold values from -0.15625 to 0.15625
- fc_m: float32 [4, 8, 200, 256], P('own', 'dp'), may hold values from -0.6 to 0.6
- fc_v: float32 [4, 8, 200, 256], P('own', 'dp'), may hold values from 0.001 to 0.1
- ln_params: float32 [4, 1600], replicated, may hold values from -3 to 3
- ln_m: float32 [4, 1600], replicated, may hold values from -0.6 to 0.6
- ln_v: float32 [4, 1600], replicated, may hold values from 0.001 to 0.1
- emb_weights: bfloat16 [4, 8, 4, 1600], P('own'), may hold values from -0.29882812 to 0.29882812
- emb_m: float32 [4, 8, 4, 1600], P('own', 'dp'), may hold values from -0.6 to 0.6
- emb_v: float32 [4, 8, 4, 1600], P('own', 'dp'), may hold values from 0.001 to 0.1
- step_count: int32 [1], replicated, may hold values from 1 to 63
Outputs:
- fc_m_next: float32 [4, 8, 200, 256], P('own', 'dp')
- fc_v_next: float32 [4, 8, 200, 256], P('own', 'dp')
- fc_direction: float32 [4, 8, 200, 256], P('own', 'dp')
- weights_next: bfloat16 [4, 8, 200, 1600], P('own')
- basis_next: float32 [1600, 256], replicated
- ln_next: float32 [4, 1600], replicated
- ln_m_next: float32 [4, 1600], replicated
- ln_v_next: float32 [4, 1600], replicated
- emb_next: bfloat16 [4, 8, 4, 1600], P('own')
- emb_m_next: float32 [4, 8, 4, 1600], P('own', 'dp')
- emb_v_next: float32 [4, 8, 4, 1600], P('own', 'dp')
All inputs are finite; a program needn't handle non-finite values.
Results may differ from a plain program's by a relative error of at most 0.009.
Values may be sent and summed in bfloat16 or wider, within the bound.
No kernel may reach another device: no remote copies, remote signals or barrier semaphores. Data moves between devices by JAX's collectives and lax.ppermute only.
A program may use at most 128 MiB of HBM per device.

v0:
```python
import math

import jax
import jax.numpy as jnp
from jax import lax
from jax.sharding import PartitionSpec as P

FF = 6400
RANK = 256
NS_STEPS = 5


beta_one = 0.9
beta_two = 0.999
adam_eps = 1e-08
learn_rate = 0.02
galore_scale = 0.25


def adam_update(moment_one, moment_two, gradient, correct_one, correct_two):
    moment_one_new = beta_one * moment_one + (1.0 - beta_one) * gradient
    moment_two_new = beta_two * moment_two + (1.0 - beta_two) * gradient * gradient
    direction = moment_one_new / correct_one / (jnp.sqrt(moment_two_new / correct_two) + adam_eps)
    return (moment_one_new, moment_two_new, direction)


def orthogonalize(subspace):
    highest = lax.Precision.HIGHEST
    iterate = subspace * lax.rsqrt(jnp.sum(subspace * subspace) + 1e-06)
    for sweep_index in range(NS_STEPS):
        gram_matrix = jnp.dot(iterate.T, iterate, precision=highest)
        iterate = 1.5 * iterate - 0.5 * jnp.dot(iterate, gram_matrix, precision=highest)
    return iterate


def shards(
    grads_fc,
    grads_ln,
    grads_emb,
    weights_fc,
    basis,
    fc_m,
    fc_v,
    ln_params,
    ln_m,
    ln_v,
    emb_weights,
    emb_m,
    emb_v,
    step_count,
):
    highest = lax.Precision.HIGHEST
    replicas = lax.axis_size("dp")
    owners = lax.axis_size("own")
    replica = lax.axis_index("dp")
    row_count = grads_fc.shape[3]
    width = grads_fc.shape[4]
    rank_cols = basis.shape[1]
    emb_count = grads_emb.shape[3]
    fc_part, emb_part = (
        lax.psum_scatter(
            grads_fc.astype(jnp.float32).astype(jnp.bfloat16), "dp", scatter_dimension=2, tiled=True
        ).astype(jnp.float32),
        lax.psum_scatter(
            grads_emb.astype(jnp.float32).astype(jnp.bfloat16),
            "dp",
            scatter_dimension=2,
            tiled=True,
        ).astype(jnp.float32),
    )
    ln_sum = lax.psum(grads_ln.astype(jnp.float32), "dp").reshape(4, width)
    fc_rows = fc_part.reshape(row_count, width)
    proj_rows = jnp.dot(fc_rows, basis, precision=highest)
    partial_value = jnp.dot(fc_rows.T, proj_rows, precision=highest)
    emb_rows = emb_part.reshape(1, 1, emb_count, width)
    proj_square = jnp.sum(proj_rows * proj_rows)
    emb_square = jnp.sum(emb_rows * emb_rows)
    subspace, proj_total, emb_total = lax.psum(
        (partial_value, proj_square, emb_square), ("dp", "own")
    )
    grad_norm = jnp.sqrt(proj_total + emb_total + jnp.sum(ln_sum * ln_sum) + 1e-06)
    clip_limit = math.sqrt(FF * RANK + emb_count * replicas * owners * width + 4 * width)
    factor = jnp.minimum(1.0, clip_limit / grad_norm)
    count = step_count[0].astype(jnp.float32)
    correct_one = 1.0 - jnp.power(jnp.float32(beta_one), count)
    correct_two = 1.0 - jnp.power(jnp.float32(beta_two), count)
    fc_grad = factor * proj_rows.reshape(1, 1, row_count, rank_cols)
    fc_m_next, fc_v_next, fc_direction = adam_update(fc_m, fc_v, fc_grad, correct_one, correct_two)
    ln_m_next, ln_v_next, ln_direction = adam_update(
        ln_m, ln_v, factor * ln_sum, correct_one, correct_two
    )
    ln_next = ln_params - learn_rate * ln_direction
    emb_m_next, emb_v_next, emb_direction = adam_update(
        emb_m, emb_v, factor * emb_rows, correct_one, correct_two
    )
    emb_mine = lax.dynamic_index_in_dim(emb_weights[0], replica, 0, keepdims=False)
    emb_new_rows = (
        emb_mine.astype(jnp.float32) - learn_rate * emb_direction.reshape(emb_count, width)
    ).astype(jnp.bfloat16)
    emb_new_rows = emb_new_rows.reshape(1, 1, emb_count, width)
    weights_mine = lax.dynamic_index_in_dim(weights_fc[0], replica, 0, keepdims=False)
    update_rows = jnp.dot(fc_direction.reshape(row_count, rank_cols), basis.T, precision=highest)
    new_rows = (weights_mine.astype(jnp.float32) - learn_rate * galore_scale * update_rows).astype(
        jnp.bfloat16
    )
    weights_next, emb_next = (
        lax.all_gather(new_rows.reshape(1, 1, row_count, width), "dp", axis=1, tiled=True),
        lax.all_gather(emb_new_rows, "dp", axis=1, tiled=True),
    )
    basis_next = orthogonalize(subspace)
    return (
        fc_m_next,
        fc_v_next,
        fc_direction,
        weights_next,
        basis_next,
        ln_next,
        ln_m_next,
        ln_v_next,
        emb_next,
        emb_m_next,
        emb_v_next,
    )


def solution(mesh):
    in_specs = (
        P("dp", "own", None, None, None),
        P("dp", None, None),
        P("dp", "own", None, None, None),
        P("own", None, None, None),
        P(),
        P("own", "dp", None, None),
        P("own", "dp", None, None),
        P(),
        P(),
        P(),
        P("own", None, None, None),
        P("own", "dp", None, None),
        P("own", "dp", None, None),
        P(),
    )
    out_specs = (
        P("own", "dp", None, None),
        P("own", "dp", None, None),
        P("own", "dp", None, None),
        P("own", None, None, None),
        P(),
        P(),
        P(),
        P(),
        P("own", None, None, None),
        P("own", "dp", None, None),
        P("own", "dp", None, None),
    )
    return jax.shard_map(shards, mesh=mesh, in_specs=in_specs, out_specs=out_specs, check_vma=False)
```

profile of v0, /device:TPU:0, one launch (start us, length us, event | category | flops | bytes accessed | tf_op | source)
XLA Modules:
  0.0 450.5 jit_solution(5772148660004264576)
XLA Ops:
  7.2 0.0 copy-start
  7.2 0.0 reduce-scatter.6.cloned.1.call-start
  7.2 0.7 reduce-scatter.6.cloned.1.call-update
  7.9 0.0 all-reduce.7.cloned.1.call-start
  8.0 0.7 all-reduce.7.cloned.1.call-update
  8.7 0.0 all-reduce.5.cloned.1.call-start
  8.7 129.6 %reduce-scatter.6.cloned.1.call-done = bf16[1,1,1,200,1600]{4,3,2,1,0:T(8,128)(2,1)} async-done(((bf16[1,1,8,200,1600]{4,3,2,1,0:T(8,128)(2,1)}), bf16[1,1,1,200,1600]{4,3,2,1,0:T(8,128)(2,1)}) %reduce-scatter.6.cloned.1.call-update) | async-done | bytes 640016
  138.4 0.0 copy-done
  138.4 0.0 copy-start.2
  138.4 2.7 multiply_reduce_fusion.1
  141.1 0.0 copy-done.2
  141.1 0.0 copy-start.12
  141.1 0.0 copy-start.11
  141.1 0.0 copy-start.4
  141.1 0.0 copy-start.5
  141.1 2.2 convolution_bitcast_fusion
  143.3 0.0 all-reduce.5.cloned.1.call-update
  143.3 0.0 all-gather.3.cloned.1.call-start
  144.1 0.0 copy-done.12
  144.1 0.6 dynamic-slice.2
  144.7 0.0 copy-done.11
  144.7 35.3 %psum.30 = f32[1,4,1600]{2,1,0:T(4,128)S(1)} all-reduce(bf16[1,4,1600]{2,1,0:T(4,128)(2,1)S(1)} %copy-done.11), channel_id=1, replica_groups=mesh['dp'=8,'own'=4] {'dp'}, use_global_device_ids=true, to_apply=%region_6.0 | all-reduce | flops 6400 | bytes 38400 | tf_op jit(solution)/shard_map/psum | solution.py:71
  179.9 0.6 multiply_reduce_fusion.2
  180.6 29.6 %all-reduce.7.cloned.1.call-done = bf16[1,1,8,4,1600]{4,3,2,1,0:T(4,128)(2,1)} async-done(((bf16[1,1,8,4,1600]{4,3,2,1,0:T(4,128)(2,1)}), bf16[1,1,8,4,1600]{4,3,2,1,0:T(4,128)(2,1)}) %all-reduce.7.cloned.1.call-update) | async-done | bytes 102416
  210.2 2.0 fusion.18
  213.4 40.6 %psum.32 = f32[]{:T(128)} all-reduce(f32[]{:T(128)S(6)} %add.66), channel_id=1, replica_groups=mesh['dp'=8,'own'=4] {'dp','own'}, use_global_device_ids=true, to_apply=%region_2.0 | all-reduce | flops 1 | bytes 8 | tf_op jit(solution)/shard_map/psum | solution.py:78
  255.4 0.0 copy-done.4
  255.4 0.0 copy-done.5
  255.4 0.9 multiply_divide_fusion
  256.3 0.0 copy-start.3
  256.3 0.0 copy-start.6
  256.3 0.0 copy-start.7
  256.3 0.0 copy-start.8
  256.3 0.0 copy-start.9
  256.3 0.0 copy-start.10
  256.3 3.8 fusion.6
  260.1 0.0 all-gather.3.cloned.1.call-update
  260.1 0.0 copy-done.3
  260.2 0.0 copy-done.6
  260.2 0.0 copy-done.7
  260.2 2.0 fusion.25
  262.2 30.7 %all_gather.7 = bf16[1,8,4,1600]{3,2,0,1:T(4,128)(2,1)S(1)} all-gather(bf16[1,1,4,1600]{3,2,0,1:T(4,128)(2,1)S(1)} %get-tuple-element.22), channel_id=1, replica_groups=mesh['dp'=8,'own'=4] {'dp'}, dimensions={1}, use_global_device_ids=true | all-gather | bytes 115200 | tf_op jit(solution)/shard_map/all_gather | solution.py:108
  292.9 0.0 copy-done.8
  292.9 0.0 copy-done.9
  292.9 0.0 copy-done.10
  292.9 0.7 multiply_subtract_fusion
  293.6 54.7 %all-reduce.5.cloned.1.call-done = f32[1600,256]{1,0:T(8,128)} async-done(((f32[1600,256]{1,0:T(8,128)}), f32[1600,256]{1,0:T(8,128)}) %all-reduce.5.cloned.1.call-update) | async-done | bytes 1638416 | tf_op jit(solution)/shard_map/psum | solution.py:78
  348.3 0.0 copy-start.1
  348.3 2.6 multiply_reduce_fusion
  351.5 0.0 copy-done.1
  351.5 2.9 fusion.7
  354.5 1.6 fusion.4
  356.0 3.0 fusion.31
  359.0 1.5 fusion.3
  360.5 3.2 fusion.32
  363.7 1.5 fusion.2
  365.2 3.0 fusion.33
  368.2 1.5 fusion.1
  369.7 3.0 fusion.34
  372.7 2.7 fusion
  375.4 62.7 %all-gather.3.cloned.1.call-done = bf16[1600,1600]{1,0:T(8,128)(2,1)} async-done(((bf16[200,1600]{1,0:T(8,128)(2,1)}), bf16[1600,1600]{1,0:T(8,128)(2,1)}) %all-gather.3.cloned.1.call-update) | async-done | bytes 5120016 | tf_op jit(solution)/shard_map/all_gather | solution.py:107
  438.1 5.3 %copy.37 = bf16[1,8,200,1600]{3,2,1,0:T(8,128)(2,1)} copy(bf16[1,8,200,1600]{3,2,1,0:T(8,128)(2,1)} %bitcast.73) | data formatting | bytes 10240000
  443.3 0.6 copy.38
Async XLA Ops:
  7.2 131.2 %copy-start = (f32[1600,256]{1,0:T(8,128)S(1)}, f32[1600,256]{1,0:T(8,128)}, u32[]{:S(2)}) copy-start(f32[1600,256]{1,0:T(8,128)} %param.18) | copy-start | bytes 4915204
  7.2 131.2 %reduce-scatter.6.cloned.1.call-start = ((), (), s32[]{:S(2)}) async-start(), calls=%async_computation.4 | async-start | bytes 5990400
  7.9 202.2 %all-reduce.7.cloned.1.call-start = ((), (), s32[]{:S(2)}) async-start(), calls=%async_computation.3 | async-start | bytes 212992
  8.7 339.6 %all-reduce.5.cloned.1.call-start = ((), (), s32[]{:S(2)}) async-start(), calls=%async_computation.1 | async-start | bytes 3276800 | tf_op jit(solution)/shard_map/psum | solution.py:78
  138.4 2.7 copy-start.2
  141.1 3.0 copy-start.12
  141.1 3.6 copy-start.11
  141.1 114.3 %copy-start.4 = (f32[1,1,200,256]{3,2,1,0:T(8,128)S(1)}, f32[1,1,200,256]{3,2,1,0:T(8,128)}, u32[]{:S(2)}) copy-start(f32[1,1,200,256]{3,2,1,0:T(8,128)} %param.20) | copy-start | bytes 614404
  141.1 114.4 %copy-start.5 = (f32[1,1,200,256]{3,2,1,0:T(8,128)S(1)}, f32[1,1,200,256]{3,2,1,0:T(8,128)}, u32[]{:S(2)}) copy-start(f32[1,1,200,256]{3,2,1,0:T(8,128)} %param.19) | copy-start | bytes 614404
  143.3 294.8 %all-gather.3.cloned.1.call-start = ((), (), s32[]{:S(2)}) async-start(), calls=%async_computation.2 | async-start | bytes 5990400 | tf_op jit(solution)/shard_map/all_gather | solution.py:107
  256.3 3.8 copy-start.3
  256.3 3.8 copy-start.6
  256.3 3.9 copy-start.7
  256.3 36.6 %copy-start.8 = (f32[4,1600]{1,0:T(4,128)S(1)}, f32[4,1600]{1,0:T(4,128)}, u32[]{:S(2)}) copy-start(f32[4,1600]{1,0:T(4,128)} %param.21) | copy-start | bytes 76804
  256.3 36.6 %copy-start.9 = (f32[4,1600]{1,0:T(4,128)S(1)}, f32[4,1600]{1,0:T(4,128)}, u32[]{:S(2)}) copy-start(f32[4,1600]{1,0:T(4,128)} %param.23) | copy-start | bytes 76804
  256.3 36.6 %copy-start.10 = (f32[4,1600]{1,0:T(4,128)S(1)}, f32[4,1600]{1,0:T(4,128)}, u32[]{:S(2)}) copy-start(f32[4,1600]{1,0:T(4,128)} %param.22) | copy-start | bytes 76804
  348.3 3.3 copy-start.1
Sparse Core Ops, SparseCore 0:
  11.5 126.8 reduce-scatter.5
  142.1 68.0 all-reduce.6
  216.1 132.0 all-reduce.4
  351.1 86.8 all-gather.2
where the time goes:
time: 451 us
  waiting for transfers between devices  278 us (62%)
  blocking collectives  107 us (24%)
  matrix products  32.4 us (7%)
  between operations  18 us (4%)
  other arithmetic  8.74 us (2%)
  local copies, waits for them, and re-layouts  6.57 us (1%)
    unnamed x6, waiting for transfers between devices  161 us
    all_gather x1, waiting for transfers between devices, shards(): lax.all_gather(new_rows.reshape(1, 1, row_count, width), 'dp', axis=1, ti...  62.7 us
    psum x1, waiting for transfers between devices, shards(): lax.psum((partial_value, proj_square, emb_square), ('dp', 'own'))  54.7 us
    psum x1, blocking collectives, shards(): lax.psum((partial_value, proj_square, emb_square), ('dp', 'own'))  40.6 us
    psum x1, blocking collectives, shards(): ln_sum = lax.psum(grads_ln.astype(jnp.float32), 'dp').reshape(4, width)  35.3 us
    all_gather x1, blocking collectives, shards(): lax.all_gather(emb_new_rows, 'dp', axis=1, tiled=True)  30.7 us
    dot_general x5, matrix products, orthogonalize(): gram_matrix = jnp.dot(iterate.T, iterate, precision=highest)  15 us
  transfers between devices with their start and end apart: 4, of which 4 were waited for; matrix products, arithmetic and copies ran while one was open for 9% of the time, Pallas kernels for 0%

commit v1 on v0

--- a/solution.py
+++ b/solution.py
@@ -31,6 +31,53 @@
         gram_matrix = jnp.dot(iterate.T, iterate, precision=highest)
         iterate = 1.5 * iterate - 0.5 * jnp.dot(iterate, gram_matrix, precision=highest)
     return iterate
+
+
+def row_count_of(piece, cols):
+    return -(-piece.size // cols)
+
+
+def pack_rows(pieces, cols):
+    rows = []
+    for piece in pieces:
+        if piece.ndim == 2 and piece.shape[1] == cols:
+            rows.append(piece)
+            continue
+        flat = piece.reshape(-1)
+        flat = jnp.pad(flat, (0, row_count_of(piece, cols) * cols - flat.size))
+        rows.append(flat.reshape(-1, cols))
+    return jnp.concatenate(rows, axis=0)
+
+
+def unpack_rows(packed, pieces):
+    cols = packed.shape[1]
+    out = []
+    start = 0
+    for piece in pieces:
+        count = row_count_of(piece, cols)
+        block = packed[start : start + count]
+        start += count
+        out.append(block.reshape(-1)[: piece.size].reshape(piece.shape))
+    return out
+
+
+def split3(values):
+    first = values.astype(jnp.bfloat16)
+    rest = values - first.astype(jnp.float32)
+    second = rest.astype(jnp.bfloat16)
+    third = (rest - second.astype(jnp.float32)).astype(jnp.bfloat16)
+    return jnp.concatenate([first, second, third], axis=1)
+
+
+def exact_dot(lhs_bf16, rhs_f32, contract):
+    cols = rhs_f32.shape[1]
+    wide = lax.dot_general(
+        lhs_bf16,
+        split3(rhs_f32),
+        ((contract, (0,)), ((), ())),
+        preferred_element_type=jnp.float32,
+    )
+    return wide[:, :cols] + wide[:, cols : 2 * cols] + wide[:, 2 * cols :]
 
 
 def shards(
@@ -53,60 +100,62 @@
     replicas = lax.axis_size("dp")
     owners = lax.axis_size("own")
     replica = lax.axis_index("dp")
+    blocks = grads_fc.shape[2]
     row_count = grads_fc.shape[3]
     width = grads_fc.shape[4]
     rank_cols = basis.shape[1]
     emb_count = grads_emb.shape[3]
-    fc_part, emb_part = (
-        lax.psum_scatter(
-            grads_fc.astype(jnp.float32).astype(jnp.bfloat16), "dp", scatter_dimension=2, tiled=True
-        ).astype(jnp.float32),
-        lax.psum_scatter(
-            grads_emb.astype(jnp.float32).astype(jnp.bfloat16),
-            "dp",
-            scatter_dimension=2,
-            tiled=True,
-        ).astype(jnp.float32),
-    )
-    ln_sum = lax.psum(grads_ln.astype(jnp.float32), "dp").reshape(4, width)
-    fc_rows = fc_part.reshape(row_count, width)
-    proj_rows = jnp.dot(fc_rows, basis, precision=highest)
-    partial_value = jnp.dot(fc_rows.T, proj_rows, precision=highest)
-    emb_rows = emb_part.reshape(1, 1, emb_count, width)
-    proj_square = jnp.sum(proj_rows * proj_rows)
-    emb_square = jnp.sum(emb_rows * emb_rows)
-    subspace, proj_total, emb_total = lax.psum(
-        (partial_value, proj_square, emb_square), ("dp", "own")
-    )
-    grad_norm = jnp.sqrt(proj_total + emb_total + jnp.sum(ln_sum * ln_sum) + 1e-06)
+    local_rows = grads_fc.reshape(blocks * row_count, width)
+    local_proj = exact_dot(local_rows, basis, (1,))
+    emb_local = grads_emb.reshape(blocks, emb_count, width).astype(jnp.float32)
+    ln_local = grads_ln.reshape(4, width).astype(jnp.float32)
+    proj_own, emb_own, ln_sum = unpack_rows(
+        lax.psum(pack_rows((local_proj, emb_local, ln_local), rank_cols), "dp"),
+        (local_proj, emb_local, ln_local),
+    )
+    partial_value = exact_dot(local_rows, proj_own, (0,))
+    own_square = jnp.sum(proj_own * proj_own) + jnp.sum(emb_own * emb_own)
+    own_square = jnp.where(replica == 0, own_square, 0.0)
+    subspace, square_total = unpack_rows(
+        lax.psum(pack_rows((partial_value, own_square), rank_cols), ("dp", "own")),
+        (partial_value, own_square),
+    )
+    grad_norm = jnp.sqrt(square_total + jnp.sum(ln_sum * ln_sum) + 1e-06)
     clip_limit = math.sqrt(FF * RANK + emb_count * replicas * owners * width + 4 * width)
     factor = jnp.minimum(1.0, clip_limit / grad_norm)
     count = step_count[0].astype(jnp.float32)
     correct_one = 1.0 - jnp.power(jnp.float32(beta_one), count)
     correct_two = 1.0 - jnp.power(jnp.float32(beta_two), count)
+    proj_rows = lax.dynamic_slice_in_dim(proj_own, replica * row_count, row_count, 0)
     fc_grad = factor * proj_rows.reshape(1, 1, row_count, rank_cols)
     fc_m_next, fc_v_next, fc_direction = adam_update(fc_m, fc_v, fc_grad, correct_one, correct_two)
     ln_m_next, ln_v_next, ln_direction = adam_update(
         ln_m, ln_v, factor * ln_sum, correct_one, correct_two
     )
     ln_next = ln_params - learn_rate * ln_direction
+    emb_rows = lax.dynamic_index_in_dim(emb_own, replica, 0, keepdims=True).reshape(
+        1, 1, emb_count, width
+    )
     emb_m_next, emb_v_next, emb_direction = adam_update(
         emb_m, emb_v, factor * emb_rows, correct_one, correct_two
     )
-    emb_mine = lax.dynamic_index_in_dim(emb_weights[0], replica, 0, keepdims=False)
-    emb_new_rows = (
-        emb_mine.astype(jnp.float32) - learn_rate * emb_direction.reshape(emb_count, width)
+    fc_dir_mine = fc_direction.reshape(row_count, rank_cols)
+    emb_dir_mine = emb_direction.reshape(emb_count, width)
+    gathered = lax.all_gather(
+        pack_rows((fc_dir_mine, emb_dir_mine), rank_cols), "dp", axis=0, tiled=False
+    )
+    fc_dir_all, emb_dir_all = jax.vmap(
+        lambda packed: unpack_rows(packed, (fc_dir_mine, emb_dir_mine))
+    )(gathered)
+    fc_dir_all = fc_dir_all.reshape(replicas * row_count, rank_cols)
+    update_rows = jnp.dot(fc_dir_all, basis.T, precision=highest)
+    weights_next = (
+        weights_fc.astype(jnp.float32)
+        - learn_rate * galore_scale * update_rows.reshape(weights_fc.shape)
     ).astype(jnp.bfloat16)
-    emb_new_rows = emb_new_rows.reshape(1, 1, emb_count, width)
-    weights_mine = lax.dynamic_index_in_dim(weights_fc[0], replica, 0, keepdims=False)
-    update_rows = jnp.dot(fc_direction.reshape(row_count, rank_cols), basis.T, precision=highest)
-    new_rows = (weights_mine.astype(jnp.float32) - learn_rate * galore_scale * update_rows).astype(
-        jnp.bfloat16
-    )
-    weights_next, emb_next = (
-        lax.all_gather(new_rows.reshape(1, 1, row_count, width), "dp", axis=1, tiled=True),
-        lax.all_gather(emb_new_rows, "dp", axis=1, tiled=True),
-    )
+    emb_next = (
+        emb_weights.astype(jnp.float32) - learn_rate * emb_dir_all.reshape(emb_weights.shape)
+    ).astype(jnp.bfloat16)
     basis_next = orthogonalize(subspace)
     return (
         fc_m_next,

time: 451 us -> 354 us (0.78); the launches traced: 451 us -> 347 us
  blocking collectives: 107 us -> 0 us
  waiting for transfers between devices: 278 us -> 250 us
  matrix products: 32.4 us -> 51.7 us
  other arithmetic: 8.74 us -> 20.7 us
    psum x1 -> x2, waiting for transfers between devices: 54.7 us -> 228 us  [the longest x1 129 us: shards(): lax.psum(pack_rows((partial_value, own_square), rank_cols), ('dp', 'own'))]
    unnamed x6 -> x3, waiting for transfers between devices: 161 us -> 0.05 us
    psum x2 -> x0, blocking collectives: 75.9 us -> none  [the longest x1 40.6 us: shards(): lax.psum((partial_value, proj_square, emb_square), ('dp', 'own'))]
    all_gather x1, waiting for transfers between devices: 62.7 us -> 21.9 us  [shards(): lax.all_gather(pack_rows((fc_dir_mine, emb_dir_mine), rank_cols), 'dp', a...]
    all_gather x1 -> x0, blocking collectives: 30.7 us -> none  [shards(): lax.all_gather(emb_new_rows, 'dp', axis=1, tiled=True)]
    dot_general x3, matrix products: 8.65 us -> 28 us  [the longest x2 14.2 us: exact_dot(): lax.dot_general(lhs_bf16, split3(rhs_f32), ((contract, (0,)), ((), ())),...]
    unnamed x29 -> x16, local copies, waits for them, and re-layouts: 6.57 us -> 0.04 us
  transfers between devices with their start and end apart: 4 -> 3, of which waited for: 4 -> 3; matrix products, arithmetic and copies ran while one was open for 9% -> 8% of each run, Pallas kernels for 0% -> 0%
where the time goes in v1:
time: 354 us; the launch traced here: 347 us
  waiting for transfers between devices  250 us (71%)
  matrix products  51.7 us (15%)
  other arithmetic  20.7 us (6%)
  between operations  18.5 us (5%)
  local copies, waits for them, and re-layouts  5.88 us (2%)
    psum x1, waiting for transfers between devices, shards(): lax.psum(pack_rows((partial_value, own_square), rank_cols), ('dp', 'own'))  129 us
    psum x1, waiting for transfers between devices, shards(): lax.psum(pack_rows((local_proj, emb_local, ln_local), rank_cols), 'dp')  99.5 us
    all_gather x1, waiting for transfers between devices, shards(): lax.all_gather(pack_rows((fc_dir_mine, emb_dir_mine), rank_cols), 'dp', a...  21.9 us
    dot_general x5, matrix products, orthogonalize(): gram_matrix = jnp.dot(iterate.T, iterate, precision=highest)  15 us
    dot_general x2, matrix products, exact_dot(): lax.dot_general(lhs_bf16, split3(rhs_f32), ((contract, (0,)), ((), ())),...  14.2 us
    dot_general x1, matrix products, shards(): update_rows = jnp.dot(fc_dir_all, basis.T, precision=highest)  13.8 us
    dot_general x5, matrix products, orthogonalize(): jnp.dot(iterate, gram_matrix, precision=highest)  8.71 us
  transfers between devices with their start and end apart: 3, of which 3 were waited for; matrix products, arithmetic and copies ran while one was open for 8% of the time, Pallas kernels for 0%

profile of v1, /device:TPU:0, one launch (start us, length us, event | category | flops | bytes accessed | tf_op | source)
XLA Modules:
  0.0 347.1 jit_solution(15849744454099520645)
XLA Ops:
  7.2 0.0 all-reduce.4.cloned.1.call-start
  7.2 0.8 reshape.133
  8.0 1.1 reshape.132
  9.1 2.3 fusion.35
  11.3 6.5 %convolution_bitcast_fusion = f32[1600,768]{1,0:T(8,128)S(1)} fusion(bf16[1600,1600]{1,0:T(8,128)(2,1)} %bitcast.56, bf16[1600,256]{1,0:T(8,128)(2,1)S(1)} %get-tuple-element.27, bf16[1600,256]{1,0:T(8,128)(2,1)S(1)} %get-tuple-element.28, bf16[1600,256]{1,0:T(8,128)(2,1)S(1)} %get-tuple-element.26), kind=kOutput, calls=%fused_computation.2 | convolution fusion | flops 3939532800 | bytes 12492800 | tf_op jit(solution)/shard_map/dot_general | solution.py:74
  17.9 0.3 slice_add_fusion.2
  18.2 1.4 pad_maximum_fusion
  19.6 0.0 all-reduce.4.cloned.1.call-update
  19.6 0.0 all-reduce.6.cloned.1.call-start
  19.7 99.5 %all-reduce.4.cloned.1.call-done = f32[1825,256]{1,0:T(8,128)} async-done(((f32[1825,256]{1,0:T(8,128)}), f32[1825,256]{1,0:T(8,128)}) %all-reduce.4.cloned.1.call-update) | async-done | bytes 1868816 | tf_op jit(solution)/shard_map/psum | solution.py:113
  119.2 1.6 fusion.34
  120.8 2.5 fusion.20
  124.6 1.5 slice.95
  126.1 7.6 %convolution_bitcast_fusion.1 = f32[1600,768]{1,0:T(8,128)S(1)} fusion(bf16[1600,1600]{1,0:T(8,128)(2,1)} %bitcast.57, bf16[1600,256]{1,0:T(8,128)(2,1)S(1)} %get-tuple-element.24, bf16[1600,256]{1,0:T(8,128)(2,1)S(1)} %get-tuple-element.22, bf16[1600,256]{1,0:T(8,128)(2,1)S(1)} %slice.95), kind=kOutput, calls=%fused_computation.3 | convolution fusion | flops 3939532800 | bytes 12492800 | tf_op jit(solution)/shard_map/dot_general | solution.py:74
  133.7 0.3 slice_add_fusion
  134.0 1.3 pad_maximum_fusion.1
  135.3 0.0 copy-start.4
  135.3 0.0 all-reduce.6.cloned.1.call-update
  135.3 0.2 all-gather.4.cloned.1.call-start
  136.3 0.9 reshape_reshape.2
  137.2 1.4 multiply_reduce_fusion.3
  138.6 128.5 %all-reduce.6.cloned.1.call-done = f32[1601,256]{1,0:T(8,128)} async-done(((f32[1601,256]{1,0:T(8,128)}), f32[1601,256]{1,0:T(8,128)}) %all-reduce.6.cloned.1.call-update) | async-done | bytes 1639440 | tf_op jit(solution)/shard_map/psum | solution.py:120
  267.1 0.0 copy-start
  267.1 2.6 multiply_reduce_fusion
  270.4 1.2 slice.63
  272.9 0.8 slice_multiply_fusion.4
  273.7 0.1 mul.283
  273.8 0.0 copy-done.4
  273.8 1.4 multiply_divide_fusion.2
  275.2 0.1 reshape.131
  275.3 1.9 multiply_divide_fusion
  277.2 0.0 copy-start.2
  277.2 0.8 maximum_bitcast_fusion
  277.9 0.0 all-gather.4.cloned.1.call-update
  278.0 0.0 copy-done
  278.0 2.9 fusion.18
  280.9 1.5 fusion.5
  282.4 0.0 copy-done.2
  282.4 3.0 fusion.36
  285.4 1.5 fusion.4
  286.9 3.2 fusion.37
  290.1 1.5 fusion.3
  291.6 3.0 fusion.38
  294.6 1.5 fusion.2
  296.1 3.0 fusion.39
  299.1 0.0 copy-start.5
  299.1 0.0 copy-start.6
  299.2 0.0 copy-start.7
  299.2 0.0 copy-start.3
  299.2 0.0 copy-start.1
  299.2 2.7 fusion.1
  301.9 0.0 copy-done.5
  301.9 0.0 copy-done.6
  301.9 0.0 copy-done.7
  301.9 0.7 multiply_subtract_fusion
  302.5 21.9 %all-gather.4.cloned.1.call-done = f32[8,225,256]{2,1,0:T(8,128)} async-done(((f32[1,225,256]{2,1,0:T(8,128)}), f32[8,225,256]{2,1,0:T(8,128)}) %all-gather.4.cloned.1.call-update) | async-done | bytes 1843216 | tf_op jit(solution)/shard_map/all_gather | solution.py:144
  324.4 1.0 slice_multiply_fusion.3
  325.4 0.2 mul.295
  325.6 0.0 copy-done.3
  325.6 0.7 subtract_convert_fusion.2
  326.3 0.0 copy-done.1
  326.3 13.8 %fusion = bf16[1,8,200,1600]{3,2,1,0:T(8,128)(2,1)} fusion(bf16[1,8,200,1600]{3,2,1,0:T(8,128)(2,1)} %param.17, f32[8,225,256]{2,1,0:T(8,128)} %all-gather.4.cloned.1.call-done, f32[1600,256]{1,0:T(8,128)S(1)} %copy-done.1), kind=kOutput, calls=%fused_computation.1 | convolution fusion | flops 7874560000 | bytes 13721600 | tf_op jit(solution)/shard_map/dot_general | solution.py:151
  (1 shorter events, 0.0 us)
Async XLA Ops:
  7.2 112.0 %all-reduce.4.cloned.1.call-start = ((), (), s32[]{:S(2)}) async-start(), calls=%async_computation | async-start | bytes 3751936 | tf_op jit(solution)/shard_map/psum | solution.py:113
  19.6 247.5 %all-reduce.6.cloned.1.call-start = ((), (), s32[]{:S(2)}) async-start(), calls=%async_computation.1 | async-start | bytes 3293184 | tf_op jit(solution)/shard_map/psum | solution.py:120
  135.3 138.5 %copy-start.4 = (f32[1,1,4,1600]{3,2,1,0:T(4,128)S(1)}, f32[1,1,4,1600]{3,2,1,0:T(4,128)}, u32[]{:S(2)}) copy-start(f32[1,1,4,1600]{3,2,1,0:T(4,128)} %param.26) | copy-start | bytes 76804
  135.3 189.1 %all-gather.4.cloned.1.call-start = ((), (), s32[]{:S(2)}) async-start(), calls=%async_computation.2 | async-start | bytes 2138112 | tf_op jit(solution)/shard_map/all_gather | solution.py:144
  267.1 10.9 %copy-start = (f32[1601,256]{1,0:T(8,128)S(1)}, f32[1601,256]{1,0:T(8,128)}, u32[]{:S(2)}) copy-start(f32[1601,256]{1,0:T(8,128)} %all-reduce.6.cloned.1.call-done) | copy-start | bytes 4918276
  277.2 5.2 %copy-start.2 = (f32[1,1,200,256]{3,2,1,0:T(8,128)}, f32[1,1,200,256]{3,2,1,0:T(8,128)S(1)}, u32[]{:S(2)}) copy-start(f32[1,1,200,256]{3,2,1,0:T(8,128)S(1)} %get-tuple-element.17) | copy-start | bytes 614404
  299.1 2.7 copy-start.5
  299.1 2.7 copy-start.6
  299.2 2.7 copy-start.7
  299.2 26.5 %copy-start.3 = (bf16[1,8,4,1600]{3,2,1,0:T(4,128)(2,1)S(1)}, bf16[1,8,4,1600]{3,2,1,0:T(4,128)(2,1)}, u32[]{:S(2)}) copy-start(bf16[1,8,4,1600]{3,2,1,0:T(4,128)(2,1)} %param.24) | copy-start | bytes 307204
  299.2 27.2 %copy-start.1 = (f32[1600,256]{1,0:T(8,128)S(1)}, f32[1600,256]{1,0:T(8,128)}, u32[]{:S(2)}) copy-start(f32[1600,256]{1,0:T(8,128)} %param.18) | copy-start | bytes 4915204
Sparse Core Ops, SparseCore 0:
  19.7 99.4 all-reduce.3
  135.5 131.5 all-reduce.5
  278.1 46.3 all-gather.3
